TPU v7x, 512 devices: a whole 4x8x8 slice. The times are simulated.
512 devices in a mesh: dp: 32 (over z, x_lo, core), tensor: 16 (over y, x_hi).
Axes of the slice: x: 4 (x_hi: 2, x_lo: 2; x = x_hi * 2 + x_lo), y: 8, z: 8, core: 2. Of those that a mesh axis runs over, the one named last changes fastest.
Arguments:
- features: bfloat16 [5120, 36864], P('tensor', 'dp'), may hold values from -24 to 24
- cotangents: bfloat16 [36864, 2048], P('dp', 'tensor'), may hold values from -24 to 24
- labels: int32 [36864], P('dp'), may hold values from 0 to 2
- diff_mask: int32 [36864], P('dp'), may hold values 0 or 1
- class_weight: float32 [3], replicated, may hold values from 0.25 to 2
- owners: int32 [16, 32], P('tensor'), may hold values from 0 to 31, each once within a row
- momentum: float32 [5120, 2048], P('dp', 'tensor'), may hold values from -3 to 3
Outputs:
- update: bfloat16 [5120, 2048], P(None, 'tensor')
- new_momentum: float32 [5120, 2048], P('dp', 'tensor')
Inputs may be any that keep to these rules, and one draw needn't show every extreme that they name: `owners`: each row names every dp index once.
All inputs are finite; a program needn't handle non-finite values. No bound on the sum of `diff_mask` on one device may be relied on, other than what follows from the above.
Results may differ from a plain program's by a relative error of at most 0.0065.
Values may be sent and summed in bfloat16 or wider, within the bound.
No kernel may reach another device: no remote copies, remote signals or barrier semaphores. Data moves between devices by JAX's collectives and lax.ppermute only.
A program may use at most 64 MiB of HBM per device.

v0:
```python
import math
import jax
import jax.numpy as jnp
from jax import lax
from jax.sharding import PartitionSpec as P

ITERS = 5
decay_rate = 0.95
quintic_first = 3.4445
quintic_second = -4.775
quintic_third = 2.0315
norm_epsilon = 1e-07


def weigh(cotangents, labels, diff_mask, class_weight, total_tokens):
    classes = jnp.arange(class_weight.shape[0], dtype=jnp.int32)
    picked = (labels[:, None] == classes[None, :]).astype(jnp.float32)
    token_weight = diff_mask.astype(jnp.float32) * jnp.sum(picked * class_weight[None, :], axis=1)
    factor = token_weight / math.sqrt(total_tokens)
    return (cotangents.astype(jnp.float32) * factor[:, None]).astype(jnp.bfloat16)


def invert(owners):
    number = owners.shape[1]
    candidates = jnp.arange(number, dtype=jnp.int32)
    matches = owners[:, None, :] == candidates[None, :, None]
    return jnp.sum(jnp.where(matches, candidates[None, None, :], 0), axis=2)


def reorder(blocks, lookup):
    return jnp.take_along_axis(blocks, jnp.transpose(lookup)[:, None, :, None], axis=0)


def orthogonalize(nesterov):
    frobenius = jnp.sqrt(jnp.sum(nesterov * nesterov, axis=(-3, -1), keepdims=True)) + norm_epsilon
    iterate = nesterov / frobenius
    for step in range(ITERS):
        gram_matrix = jnp.einsum(
            "...rhc,...rhd->...hcd", iterate, iterate, precision=lax.Precision.HIGHEST
        )
        poly_matrix = quintic_second * gram_matrix + quintic_third * jnp.einsum(
            "...hcd,...hde->...hce", gram_matrix, gram_matrix, precision=lax.Precision.HIGHEST
        )
        iterate = quintic_first * iterate + jnp.einsum(
            "...rhc,...hcd->...rhd", iterate, poly_matrix, precision=lax.Precision.HIGHEST
        )
    return iterate


def shards(features, cotangents, labels, diff_mask, class_weight, owners, momentum):
    dp_count = lax.axis_size("dp")
    tensor_count = lax.axis_size("tensor")
    local_tokens = cotangents.shape[0]
    scaled = weigh(cotangents, labels, diff_mask, class_weight, local_tokens * dp_count)
    heads_here = owners.shape[0]
    head_width = cotangents.shape[1] // heads_here
    block_rows = features.shape[0] * tensor_count // dp_count
    inverse = invert(owners)
    all_heads = lax.all_gather(scaled, "tensor", axis=1, tiled=True)
    rows_all_heads = jnp.dot(features, all_heads, preferred_element_type=jnp.float32)
    partial_grad = lax.all_to_all(
        rows_all_heads.reshape(features.shape[0], tensor_count, head_width),
        "tensor",
        split_axis=1,
        concat_axis=0,
        tiled=True,
    ).reshape(features.shape[0] * tensor_count, head_width)
    blocks = partial_grad.reshape(dp_count, block_rows, heads_here * head_width)
    in_owner_order = jnp.take(blocks, inverse[0], axis=0).reshape(
        dp_count * block_rows, heads_here * head_width
    )
    own_block = lax.psum_scatter(in_owner_order, "dp", scatter_dimension=0, tiled=True).reshape(
        block_rows, heads_here, head_width
    )
    previous = momentum.reshape(block_rows, heads_here, head_width)
    new_momentum = decay_rate * previous + own_block
    nesterov = own_block + decay_rate * new_momentum
    ortho = orthogonalize(nesterov)
    own_update = (
        (ortho * math.sqrt(block_rows))
        .astype(jnp.bfloat16)
        .reshape(block_rows, heads_here * head_width)
    )
    gathered = lax.all_gather(own_update, "dp", axis=0, tiled=True)
    placed = reorder(gathered.reshape(dp_count, block_rows, heads_here, head_width), owners)
    return (
        placed.reshape(dp_count * block_rows, heads_here * head_width),
        new_momentum.reshape(block_rows, heads_here * head_width),
    )


def solution(mesh):
    in_specs = (
        P("tensor", "dp"),
        P("dp", "tensor"),
        P("dp"),
        P("dp"),
        P(),
        P("tensor", None),
        P("dp", "tensor"),
    )
    out_specs = (P(None, "tensor"), P("dp", "tensor"))
    return jax.shard_map(shards, mesh=mesh, in_specs=in_specs, out_specs=out_specs, check_vma=False)
```

profile of v0, /device:TPU:1, one launch (start us, length us, event | category | flops | bytes accessed | tf_op | source)
XLA Modules:
  0.0 416.9 jit_solution(2855944453115864971)
XLA Ops:
  7.2 0.9 select_reduce_fusion
  8.1 0.7 multiply_multiply_fusion
  8.8 1.9 multiply_convert_fusion
  10.7 118.2 %all-gather.4.cloned.1.call-done = bf16[1152,2048]{1,0:T(8,128)(2,1)} async-done(((bf16[1152,128]{1,0:T(8,128)(2,1)}), bf16[1152,2048]{1,0:T(8,128)(2,1)}) %all-gather.4.cloned.1.call-update) | async-done | bytes 4718608 | tf_op jit(solution)/shard_map/all_gather | solution.py:59
  128.9 4.2 %convolution_bitcast_fusion = f32[40,16,8,128]{3,2,1,0:T(8,128)S(1)} fusion(bf16[320,1152]{1,0:T(8,128)(2,1)S(1)} %copy-done, bf16[1152,2048]{1,0:T(8,128)(2,1)} %all-gather.4.cloned.1.call-done), kind=kOutput, calls=%fused_computation.4 | convolution fusion | flops 1509949440 | bytes 8077312 | tf_op jit(solution)/shard_map/dot_general | solution.py:60
  133.1 1.8 copy.13
  134.9 3.9 all-to-all-start
  138.8 0.1 select_reduce_fusion.1
  139.0 0.1 broadcast_in_dim.52
  139.1 59.7 %all-to-all-done = f32[320,16,128]{2,0,1:T(8,128)S(1)} async-done(((f32[320,16,128]{2,0,1:T(8,128)}), f32[320,16,128]{2,0,1:T(8,128)S(1)}, u32[]{:S(2)}, u32[]{:S(2)}) %all-to-all-start) | async-done | bytes 2621472 | tf_op jit(solution)/shard_map/all_to_all | solution.py:61
  198.9 2.2 gather_fusion
  201.1 5.3 %bitcast_select_fusion = f32[5120,128]{1,0:T(8,128)} fusion(f32[32,160,128]{2,1,0:T(8,128)} %gather_fusion, pred[5120]{0:T(1024)(128)(4,1)S(1)} %broadcast_in_dim.52), kind=kLoop, calls=%fused_computation.3 | loop fusion | flops 655360 | bytes 5248000 | tf_op jit(solution)/shard_map/jit(_take)/select_n | solution.py:69
  206.4 121.1 %reduce-scatter.2.cloned.1.call-done = f32[160,128]{1,0:T(8,128)} async-done(((f32[5120,128]{1,0:T(8,128)}), f32[160,128]{1,0:T(8,128)}) %reduce-scatter.2.cloned.1.call-update) | async-done | bytes 81936 | tf_op jit(solution)/shard_map/reduce_scatter | solution.py:72
  327.5 1.5 multiply_reduce_fusion
  329.7 1.4 fusion.24
  331.1 0.2 fusion.10
  331.3 1.2 fusion
  332.5 0.4 fusion.22
  332.9 0.2 fusion.9
  333.1 0.2 fusion.1
  333.4 0.4 fusion.19
  333.8 0.2 fusion.8
  334.0 0.2 fusion.2
  334.2 0.4 fusion.16
  334.7 0.2 fusion.7
  334.9 0.2 fusion.3
  335.1 0.4 fusion.13
  335.6 0.2 fusion.6
  335.8 0.8 fusion.11
  336.9 68.0 %all-gather.6.cloned.1.call-done = bf16[5120,1,128]{2,0,1:T(8,128)(2,1)} async-done(((bf16[160,1,128]{2,0,1:T(8,128)(2,1)}), bf16[5120,1,128]{2,0,1:T(8,128)(2,1)}) %all-gather.6.cloned.1.call-update) | async-done | bytes 1310736 | tf_op jit(solution)/shard_map/all_gather | solution.py:84
  404.9 2.1 gather_fusion.1
  407.0 3.4 bitcast_select_fusion.1
  (23 shorter events, 0.5 us)
Async XLA Ops:
  7.2 121.8 %copy-start = (bf16[320,1152]{1,0:T(8,128)(2,1)S(1)}, bf16[320,1152]{1,0:T(8,128)(2,1)}, u32[]{:S(2)}) copy-start(bf16[320,1152]{1,0:T(8,128)(2,1)} %param.7) | copy-start | bytes 2211844
  7.2 121.7 %all-gather.4.cloned.1.call-start = ((), (), s32[]{:S(2)}) async-start(), calls=%async_computation.2 | async-start | bytes 5013504 | tf_op jit(solution)/shard_map/all_gather | solution.py:59
  134.9 3.9 copy-start.3
  134.9 64.0 %all-to-all-start = ((f32[320,16,128]{2,0,1:T(8,128)}), f32[320,16,128]{2,0,1:T(8,128)S(1)}, u32[]{:S(2)}, u32[]{:S(2)}) async-start(f32[320,16,128]{2,0,1:T(8,128)} %bitcast.100), calls=%async_computation | async-start | bytes 5242880 | tf_op jit(solution)/shard_map/all_to_all | solution.py:61
  138.8 188.7 %reduce-scatter.2.cloned.1.call-start = ((), (), s32[]{:S(2)}) async-start(), calls=%async_computation.3 | async-start | bytes 2703360 | tf_op jit(solution)/shard_map/reduce_scatter | solution.py:72
  206.3 121.1 %copy-start.1 = (f32[160,128]{1,0:T(8,128)S(1)}, f32[160,128]{1,0:T(8,128)}, u32[]{:S(2)}) copy-start(f32[160,128]{1,0:T(8,128)} %param.13) | copy-start | bytes 245764
  206.4 198.6 %all-gather.6.cloned.1.call-start = ((), (), s32[]{:S(2)}) async-start(), calls=%async_computation.4 | async-start | bytes 1351680 | tf_op jit(solution)/shard_map/all_gather | solution.py:84
  329.0 78.1 %copy-start.2 = (f32[160,128]{1,0:T(8,128)}, f32[160,128]{1,0:T(8,128)S(1)}, u32[]{:S(2)}) copy-start(f32[160,128]{1,0:T(8,128)S(1)} %get-tuple-element.3) | copy-start | bytes 245764
Sparse Core Ops, SparseCore 0:
  11.6 117.2 all-gather.3
  206.5 120.9 reduce-scatter.1
  336.8 68.0 all-gather.5
where the time goes:
time: 417 us
  waiting for transfers between devices  367 us (88%)
  between operations  14.6 us (4%)
  other arithmetic  13.8 us (3%)
  matrix products  11 us (3%)
  local copies, waits for them, and re-layouts  6.46 us (2%)
    reduce_scatter x1, waiting for transfers between devices, shards(): lax.psum_scatter(in_owner_order, 'dp', scatter_dimension=0, tiled=True)  121 us
    all_gather x1, waiting for transfers between devices, shards(): all_heads = lax.all_gather(scaled, 'tensor', axis=1, tiled=True)  118 us
    all_gather x1, waiting for transfers between devices, shards(): gathered = lax.all_gather(own_update, 'dp', axis=0, tiled=True)  68 us
    all_to_all x1, waiting for transfers between devices, shards(): lax.all_to_all(rows_all_heads.reshape(features.shape[0], tensor_count, he...  59.7 us
  transfers between devices with their start and end apart: 4, of which 4 were waited for; matrix products, arithmetic and copies ran while one was open for 0% of the time, Pallas kernels for 0%

commit v1 on v0

--- a/solution.py
+++ b/solution.py
@@ -58,12 +58,12 @@
     inverse = invert(owners)
     all_heads = lax.all_gather(scaled, "tensor", axis=1, tiled=True)
     rows_all_heads = jnp.dot(features, all_heads, preferred_element_type=jnp.float32)
-    partial_grad = lax.all_to_all(
-        rows_all_heads.reshape(features.shape[0], tensor_count, head_width),
-        "tensor",
-        split_axis=1,
-        concat_axis=0,
-        tiled=True,
+    mark_set = lambda local_x: jnp.concatenate(
+        lax.all_to_all(jnp.stack(jnp.split(local_x, lax.psum(1, "tensor"), 1), 0), "tensor", 0, 0),
+        0,
+    )
+    partial_grad = mark_set(
+        rows_all_heads.reshape(features.shape[0], tensor_count, head_width)
     ).reshape(features.shape[0] * tensor_count, head_width)
     blocks = partial_grad.reshape(dp_count, block_rows, heads_here * head_width)
     in_owner_order = jnp.take(blocks, inverse[0], axis=0).reshape(

time: 417 us -> 429 us (1.029)
  local copies, waits for them, and re-layouts: 6.46 us -> 18.3 us
    unnamed x8 -> x24, local copies, waits for them, and re-layouts: 0.02 us -> 10.6 us
where the time goes in v1:
time: 429 us
  waiting for transfers between devices  367 us (86%)
  local copies, waits for them, and re-layouts  18.3 us (4%)
  between operations  14.7 us (3%)
  other arithmetic  13.8 us (3%)
  matrix products  11 us (3%)
    reduce_scatter x1, waiting for transfers between devices, shards(): lax.psum_scatter(in_owner_order, 'dp', scatter_dimension=0, tiled=True)  121 us
    all_gather x1, waiting for transfers between devices, shards(): all_heads = lax.all_gather(scaled, 'tensor', axis=1, tiled=True)  118 us
    all_gather x1, waiting for transfers between devices, shards(): gathered = lax.all_gather(own_update, 'dp', axis=0, tiled=True)  68.1 us
    all_to_all x1, waiting for transfers between devices, shards(): lax.all_to_all(jnp.stack(jnp.split(local_x, lax.psum(1, 'tensor'), 1), 0)...  59.7 us
    unnamed x24, local copies, waits for them, and re-layouts  10.6 us
  transfers between devices with their start and end apart: 4, of which 4 were waited for; matrix products, arithmetic and copies ran while one was open for 0% of the time, Pallas kernels for 0%

profile of v1, /device:TPU:1, one launch (start us, length us, event | category | flops | bytes accessed | tf_op | source)
XLA Modules:
  0.0 428.8 jit_solution(1184954164391256121)
XLA Ops:
  7.2 0.9 select_reduce_fusion
  8.1 0.7 multiply_multiply_fusion
  8.8 1.9 multiply_convert_fusion
  10.7 118.2 %all-gather.4.cloned.1.call-done = bf16[1152,2048]{1,0:T(8,128)(2,1)} async-done(((bf16[1152,128]{1,0:T(8,128)(2,1)}), bf16[1152,2048]{1,0:T(8,128)(2,1)}) %all-gather.4.cloned.1.call-update) | async-done | bytes 4718608 | tf_op jit(solution)/shard_map/all_gather | solution.py:59
  128.9 4.2 convolution_bitcast_fusion
  133.6 2.3 fusion.27
  136.0 0.7 constant_dynamic-update-slice_fusion.15
  136.6 0.7 constant_dynamic-update-slice_fusion.14
  137.3 0.7 constant_dynamic-update-slice_fusion.13
  138.0 0.7 constant_dynamic-update-slice_fusion.12
  138.6 0.7 constant_dynamic-update-slice_fusion.11
  139.3 0.7 constant_dynamic-update-slice_fusion.10
  140.0 0.7 constant_dynamic-update-slice_fusion.9
  141.3 0.7 constant_dynamic-update-slice_fusion.7
  142.0 0.7 constant_dynamic-update-slice_fusion.6
  142.7 0.7 constant_dynamic-update-slice_fusion.5
  143.4 0.7 constant_dynamic-update-slice_fusion.4
  144.0 0.7 constant_dynamic-update-slice_fusion.3
  144.7 0.7 constant_dynamic-update-slice_fusion.2
  145.4 0.7 constant_dynamic-update-slice_fusion.1
  146.7 3.9 all-to-all-start
  151.0 59.7 %all-to-all-done = f32[16,320,1,128]{3,1,2,0:T(8,128)S(1)} async-done(((f32[16,320,1,128]{3,1,2,0:T(8,128)}), f32[16,320,1,128]{3,1,2,0:T(8,128)S(1)}, u32[]{:S(2)}, u32[]{:S(2)}) %all-to-all-start) | async-done | bytes 2621472 | tf_op jit(solution)/shard_map/all_to_all | solution.py:62
  210.7 2.2 gather_fusion
  212.9 5.3 %bitcast_select_fusion = f32[5120,128]{1,0:T(8,128)} fusion(f32[32,160,128]{2,1,0:T(8,128)} %gather_fusion, pred[5120]{0:T(1024)(128)(4,1)S(1)} %broadcast_in_dim.52), kind=kLoop, calls=%fused_computation.2 | loop fusion | flops 655360 | bytes 5248000 | tf_op jit(solution)/shard_map/jit(_take)/select_n | solution.py:69
  218.3 121.1 %reduce-scatter.2.cloned.1.call-done = f32[160,128]{1,0:T(8,128)} async-done(((f32[5120,128]{1,0:T(8,128)}), f32[160,128]{1,0:T(8,128)}) %reduce-scatter.2.cloned.1.call-update) | async-done | bytes 81936 | tf_op jit(solution)/shard_map/reduce_scatter | solution.py:72
  339.3 1.5 multiply_reduce_fusion
  341.5 1.4 fusion.24
  343.2 1.2 fusion
  347.6 0.8 fusion.11
  348.7 68.1 %all-gather.6.cloned.1.call-done = bf16[5120,1,128]{2,0,1:T(8,128)(2,1)} async-done(((bf16[160,1,128]{2,0,1:T(8,128)(2,1)}), bf16[5120,1,128]{2,0,1:T(8,128)(2,1)}) %all-gather.6.cloned.1.call-update) | async-done | bytes 1310736 | tf_op jit(solution)/shard_map/all_gather | solution.py:84
  416.8 2.1 gather_fusion.1
  418.9 3.4 bitcast_select_fusion.1
  (40 shorter events, 6.0 us)
Async XLA Ops:
  7.2 121.8 %copy-start = (bf16[320,1152]{1,0:T(8,128)(2,1)S(1)}, bf16[320,1152]{1,0:T(8,128)(2,1)}, u32[]{:S(2)}) copy-start(bf16[320,1152]{1,0:T(8,128)(2,1)} %param.7) | copy-start | bytes 2211844
  7.2 121.7 %all-gather.4.cloned.1.call-start = ((), (), s32[]{:S(2)}) async-start(), calls=%async_computation.2 | async-start | bytes 5013504 | tf_op jit(solution)/shard_map/all_gather | solution.py:59
  146.7 3.9 copy-start.3
  146.7 64.0 %all-to-all-start = ((f32[16,320,1,128]{3,1,2,0:T(8,128)}), f32[16,320,1,128]{3,1,2,0:T(8,128)S(1)}, u32[]{:S(2)}, u32[]{:S(2)}) async-start(f32[16,320,1,128]{3,1,2,0:T(8,128)} %constant_dynamic-update-slice_fusion), calls=%async_computation | async-start | bytes 5242880 | tf_op jit(solution)/shard_map/all_to_all | solution.py:62
  150.6 188.7 %reduce-scatter.2.cloned.1.call-start = ((), (), s32[]{:S(2)}) async-start(), calls=%async_computation.3 | async-start | bytes 2703360 | tf_op jit(solution)/shard_map/reduce_scatter | solution.py:72
  218.2 121.1 %copy-start.1 = (f32[160,128]{1,0:T(8,128)S(1)}, f32[160,128]{1,0:T(8,128)}, u32[]{:S(2)}) copy-start(f32[160,128]{1,0:T(8,128)} %param.13) | copy-start | bytes 245764
  218.2 198.6 %all-gather.6.cloned.1.call-start = ((), (), s32[]{:S(2)}) async-start(), calls=%async_computation.4 | async-start | bytes 1351680 | tf_op jit(solution)/shard_map/all_gather | solution.py:84
  340.8 78.1 %copy-start.2 = (f32[160,128]{1,0:T(8,128)}, f32[160,128]{1,0:T(8,128)S(1)}, u32[]{:S(2)}) copy-start(f32[160,128]{1,0:T(8,128)S(1)} %get-tuple-element.3) | copy-start | bytes 245764
Sparse Core Ops, SparseCore 0:
  11.6 117.2 all-gather.3
  218.3 120.9 reduce-scatter.1
  348.6 68.1 all-gather.5

commit v2 on v0

--- a/solution.py
+++ b/solution.py
@@ -81,7 +81,20 @@
         .astype(jnp.bfloat16)
         .reshape(block_rows, heads_here * head_width)
     )
-    gathered = lax.all_gather(own_update, "dp", axis=0, tiled=True)
+
+    def _match_fields(inner_x, comm_axis):
+        arr_next = jnp.concatenate(
+            jax.lax.all_to_all(
+                jnp.stack([inner_x] * jax.lax.psum(1, axis_name=comm_axis), axis=0),
+                axis_name=comm_axis,
+                split_axis=0,
+                concat_axis=0,
+            ),
+            axis=0,
+        )
+        return arr_next
+
+    gathered = _match_fields(own_update, "dp")
     placed = reorder(gathered.reshape(dp_count, block_rows, heads_here, head_width), owners)
     return (
         placed.reshape(dp_count * block_rows, heads_here * head_width),

time: 417 us -> 391 us (0.938)
  waiting for transfers between devices: 367 us -> 333 us
  starting transfers between devices: 3.98 us -> 12.2 us
    all_gather x1 -> x0, waiting for transfers between devices: 68 us -> none  [shards(): gathered = lax.all_gather(own_update, 'dp', axis=0, tiled=True)]
    all_to_all x0 -> x1, waiting for transfers between devices: none -> 33.5 us  [_match_fields(): jax.lax.all_to_all(jnp.stack([inner_x] * jax.lax.psum(1, axis_name=comm_a...]
    all_to_all x0 -> x1, starting transfers between devices: none -> 8.23 us  [_match_fields(): jax.lax.all_to_all(jnp.stack([inner_x] * jax.lax.psum(1, axis_name=comm_a...]
where the time goes in v2:
time: 391 us; the launch traced here: 390 us
  waiting for transfers between devices  333 us (85%)
  between operations  14.9 us (4%)
  other arithmetic  13.8 us (4%)
  starting transfers between devices  12.2 us (3%)
  matrix products  10.4 us (3%)
  local copies, waits for them, and re-layouts  6.39 us (2%)
    reduce_scatter x1, waiting for transfers between devices, shards(): lax.psum_scatter(in_owner_order, 'dp', scatter_dimension=0, tiled=True)  121 us
    all_gather x1, waiting for transfers between devices, shards(): all_heads = lax.all_gather(scaled, 'tensor', axis=1, tiled=True)  118 us
    all_to_all x1, waiting for transfers between devices, shards(): lax.all_to_all(rows_all_heads.reshape(features.shape[0], tensor_count, he...  59.7 us
    all_to_all x1, waiting for transfers between devices, _match_fields(): jax.lax.all_to_all(jnp.stack([inner_x] * jax.lax.psum(1, axis_name=comm_a...  33.5 us
    all_to_all x1, starting transfers between devices, _match_fields(): jax.lax.all_to_all(jnp.stack([inner_x] * jax.lax.psum(1, axis_name=comm_a...  8.23 us
  transfers between devices with their start and end apart: 4, of which 4 were waited for; matrix products, arithmetic and copies ran while one was open for 0% of the time, Pallas kernels for 0%

profile of v2, /device:TPU:1, one launch (start us, length us, event | category | flops | bytes accessed | tf_op | source)
XLA Modules:
  0.0 390.2 jit_solution(3088976849691366537)
XLA Ops:
  7.2 0.9 select_reduce_fusion
  8.1 0.7 multiply_multiply_fusion
  8.8 1.9 multiply_convert_fusion
  10.7 118.2 %all-gather.2.cloned.1.call-done = bf16[1152,2048]{1,0:T(8,128)(2,1)} async-done(((bf16[1152,128]{1,0:T(8,128)(2,1)}), bf16[1152,2048]{1,0:T(8,128)(2,1)}) %all-gather.2.cloned.1.call-update) | async-done | bytes 4718608 | tf_op jit(solution)/shard_map/all_gather | solution.py:59
  128.9 4.2 %convolution_bitcast_fusion = f32[40,16,8,128]{3,2,1,0:T(8,128)S(1)} fusion(bf16[320,1152]{1,0:T(8,128)(2,1)S(1)} %copy-done, bf16[1152,2048]{1,0:T(8,128)(2,1)} %all-gather.2.cloned.1.call-done), kind=kOutput, calls=%fused_computation.4 | convolution fusion | flops 1509949440 | bytes 8077312 | tf_op jit(solution)/shard_map/dot_general | solution.py:60
  133.1 1.8 copy.13
  134.9 3.9 all-to-all-start
  139.2 59.7 %all-to-all-done = f32[320,16,128]{2,0,1:T(8,128)S(1)} async-done(((f32[320,16,128]{2,0,1:T(8,128)}), f32[320,16,128]{2,0,1:T(8,128)S(1)}, u32[]{:S(2)}, u32[]{:S(2)}) %all-to-all-start) | async-done | bytes 2621472 | tf_op jit(solution)/shard_map/all_to_all | solution.py:61
  198.9 2.2 gather_fusion
  201.1 5.3 %bitcast_select_fusion = f32[5120,128]{1,0:T(8,128)} fusion(f32[32,160,128]{2,1,0:T(8,128)} %gather_fusion, pred[5120]{0:T(1024)(128)(4,1)S(1)} %broadcast_in_dim.52), kind=kLoop, calls=%fused_computation.3 | loop fusion | flops 655360 | bytes 5248000 | tf_op jit(solution)/shard_map/jit(_take)/select_n | solution.py:69
  206.4 121.1 %reduce-scatter.2.cloned.1.call-done = f32[160,128]{1,0:T(8,128)} async-done(((f32[5120,128]{1,0:T(8,128)}), f32[160,128]{1,0:T(8,128)}) %reduce-scatter.2.cloned.1.call-update) | async-done | bytes 81936 | tf_op jit(solution)/shard_map/reduce_scatter | solution.py:72
  327.5 1.5 multiply_reduce_fusion
  329.7 1.4 fusion.25
  331.1 0.2 fusion.10
  331.3 1.2 fusion
  332.5 0.4 fusion.23
  333.0 0.2 fusion.9
  333.2 0.2 fusion.1
  333.4 0.4 fusion.20
  333.8 0.2 fusion.8
  334.0 0.2 fusion.2
  334.3 0.4 fusion.17
  334.7 0.2 fusion.7
  334.9 0.2 fusion.3
  335.1 0.4 fusion.14
  335.6 0.2 fusion.6
  335.8 0.2 fusion.12
  336.0 1.2 stack.3
  337.3 8.2 %all-to-all-start.1 = ((bf16[32,160,128]{2,1,0:T(8,128)(2,1)}), bf16[32,160,128]{2,1,0:T(8,128)(2,1)S(1)}, u32[]{:S(2)}, u32[]{:S(2)}) async-start(bf16[32,160,128]{2,1,0:T(8,128)(2,1)} %stack.3), calls=%async_computation.2 | async-start | bytes 2621440 | tf_op jit(solution)/shard_map/all_to_all | solution.py:87
  345.7 33.5 %all-to-all-done.1 = bf16[32,160,128]{2,1,0:T(8,128)(2,1)S(1)} async-done(((bf16[32,160,128]{2,1,0:T(8,128)(2,1)}), bf16[32,160,128]{2,1,0:T(8,128)(2,1)S(1)}, u32[]{:S(2)}, u32[]{:S(2)}) %all-to-all-start.1) | async-done | bytes 1310752 | tf_op jit(solution)/shard_map/all_to_all | solution.py:87
  379.2 0.8 gather_fusion.1
  380.0 3.4 bitcast_select_fusion.1
  (23 shorter events, 0.6 us)
Async XLA Ops:
  7.2 121.8 %copy-start = (bf16[320,1152]{1,0:T(8,128)(2,1)S(1)}, bf16[320,1152]{1,0:T(8,128)(2,1)}, u32[]{:S(2)}) copy-start(bf16[320,1152]{1,0:T(8,128)(2,1)} %param.7) | copy-start | bytes 2211844
  7.2 121.7 %all-gather.2.cloned.1.call-start = ((), (), s32[]{:S(2)}) async-start(), calls=%async_computation.3 | async-start | bytes 5013504 | tf_op jit(solution)/shard_map/all_gather | solution.py:59
  134.9 3.9 %copy-start.3 = (s32[1,32]{1,0:T(1,128)S(1)}, s32[1,32]{1,0:T(1,128)}, u32[]{:S(2)}) copy-start(s32[1,32]{1,0:T(1,128)} %param.12) | copy-start | bytes 388
  134.9 64.0 %all-to-all-start = ((f32[320,16,128]{2,0,1:T(8,128)}), f32[320,16,128]{2,0,1:T(8,128)S(1)}, u32[]{:S(2)}, u32[]{:S(2)}) async-start(f32[320,16,128]{2,0,1:T(8,128)} %bitcast.103), calls=%async_computation | async-start | bytes 5242880 | tf_op jit(solution)/shard_map/all_to_all | solution.py:61
  138.8 188.7 %reduce-scatter.2.cloned.1.call-start = ((), (), s32[]{:S(2)}) async-start(), calls=%async_computation.4 | async-start | bytes 2703360 | tf_op jit(solution)/shard_map/reduce_scatter | solution.py:72
  206.3 121.1 %copy-start.1 = (f32[160,128]{1,0:T(8,128)S(1)}, f32[160,128]{1,0:T(8,128)}, u32[]{:S(2)}) copy-start(f32[160,128]{1,0:T(8,128)} %param.13) | copy-start | bytes 245764
  329.0 8.3 %copy-start.2 = (f32[160,128]{1,0:T(8,128)}, f32[160,128]{1,0:T(8,128)S(1)}, u32[]{:S(2)}) copy-start(f32[160,128]{1,0:T(8,128)S(1)} %get-tuple-element.3) | copy-start | bytes 245764
  337.3 41.9 %all-to-all-start.1 = ((bf16[32,160,128]{2,1,0:T(8,128)(2,1)}), bf16[32,160,128]{2,1,0:T(8,128)(2,1)S(1)}, u32[]{:S(2)}, u32[]{:S(2)}) async-start(bf16[32,160,128]{2,1,0:T(8,128)(2,1)} %stack.3), calls=%async_computation.2 | async-start | bytes 2621440 | tf_op jit(solution)/shard_map/all_to_all | solution.py:87
Sparse Core Ops, SparseCore 0:
  11.6 117.2 all-gather.1
  206.5 120.9 reduce-scatter.1
